TPU v7x, 32 devices: a whole 2x2x4 slice. The times are simulated.
32 devices in a mesh: row: 4 (over z), col: 4 (over y, x), seq: 2 (over core).
Axes of the slice: x: 2, y: 2, z: 4, core: 2. Of those that a mesh axis runs over, the one named last changes fastest.
Arguments:
- tokens: bfloat16 [32, 12288], P(('col', 'seq'), 'row'), may hold values from -6 to 6
- cotangent: bfloat16 [32, 12288], P(('col', 'seq'), 'row'), may hold values from -6 to 6
- up_values: bfloat16 [4, 8, 576, 128, 128], P('row', ('col', 'seq')), may hold values from -0.109375 to 0.109375
- up_index: int32 [4, 8, 576], P('row', ('col', 'seq')), may hold values from 0 to 1151, as said below
- up_count: int32 [4, 8], P('row', ('col', 'seq')), may hold values from 144 to 576, as said below
- down_values: bfloat16 [4, 8, 576, 128, 128], P('row', ('col', 'seq')), may hold values from -0.0546875 to 0.0546875
- down_index: int32 [4, 8, 576], P('row', ('col', 'seq')), may hold values from 0 to 1151, as said below
- down_count: int32 [4, 8], P('row', ('col', 'seq')), may hold values from 144 to 576, as said below
Outputs:
- output: bfloat16 [32, 12288], P(('col', 'seq'), 'row')
- grad_tokens: bfloat16 [32, 12288], P(('col', 'seq'), 'row')
Inputs may be any that keep to these rules, and one draw needn't show every extreme that they name: `up_index`: in every tile, the slots below its count hold distinct block numbers, block row within the tile times 48 plus block column; later slots hold block numbers too and are unused. `down_index`: in every tile, the slots below its count hold distinct block numbers, block row along the model width times 48 plus block column along the hidden units; later slots hold block numbers too and are unused. `up_count`: some tile has exactly 576 nonzero blocks. `down_count`: some tile has exactly 576 nonzero blocks.
All inputs are finite; a program needn't handle non-finite values.
Results may differ from a plain program's by a relative error of at most 0.0049.
Values may be sent and summed in bfloat16 or wider, within the bound.
No kernel may reach another device: no remote copies, remote signals or barrier semaphores. Data moves between devices by JAX's collectives and lax.ppermute only.
A program may use at most 128 MiB of HBM per device.

v0:
```python
import jax
import jax.numpy as jnp
from jax import lax
from jax.experimental import pallas as pl
from jax.experimental.pallas import tpu as pltpu
from jax.sharding import PartitionSpec as P

FF = 49152


def gelu_forward(inputs):
    return jax.nn.gelu(inputs, approximate=True)


def gelu_backward(pre_act, gradient):
    return jax.vjp(gelu_forward, pre_act)[1](gradient)[0]


def activate(paired):
    pre_act = paired[0]
    return jnp.stack(
        [
            gelu_forward(pre_act).astype(jnp.bfloat16),
            gelu_backward(pre_act, paired[1]).astype(jnp.bfloat16),
        ]
    )


def group_size(slots):
    best = 1
    for size in range(1, 97):
        if slots % size == 0:
            best = size
    return best


def block_kernel(group, block_cols, pick_row, flips):
    def kernel(codes0, codes1, counts, x0, x1, w0, w1, o0, o1):
        step = pl.program_id(0)
        first = step * group

        @pl.when(step == 0)
        def _():
            o0[...] = jnp.zeros_like(o0)
            o1[...] = jnp.zeros_like(o1)

        streams = ((codes0, x0, w0, o0, flips[0], 0), (codes1, x1, w1, o1, flips[1], 1))
        for codes, x, w, o, flipped, which in streams:
            live = counts[which]

            @pl.when(first < live)
            def _(codes=codes, x=x, w=w, o=o, flipped=flipped, live=live):
                for j in range(group):
                    slot = first + j
                    code = codes[slot]
                    row = lax.div(code, block_cols)
                    col = code - row * block_cols
                    src = x[row if pick_row else col]
                    blk = w[j]
                    if flipped:
                        prod = lax.dot_general(
                            src, blk, (((1,), (1,)), ((), ())),
                            preferred_element_type=jnp.float32,
                        )
                    else:
                        prod = jnp.dot(src, blk, preferred_element_type=jnp.float32)
                    scale = jnp.where(slot < live, 1.0, 0.0).astype(jnp.float32)
                    dst = col if pick_row else row
                    o[dst] = o[dst] + prod * scale

    return kernel


def block_pass(x0, w0, codes0, x1, w1, codes1, counts, block_cols, pick_row, out_blocks, flips):
    slots, blk, _ = w0.shape
    rows = x0.shape[1]
    group = group_size(slots)

    def w_map(which):
        def index_map(i, c0, c1, c):
            last = jnp.maximum(c[which] - 1, 0) // group
            return (jnp.minimum(i, last), 0, 0)

        return index_map

    def whole(shape):
        return pl.BlockSpec(shape, lambda i, c0, c1, c: (0, 0, 0))

    spec = pltpu.PrefetchScalarGridSpec(
        num_scalar_prefetch=3,
        grid=(slots // group,),
        in_specs=[
            whole(x0.shape),
            whole(x1.shape),
            pl.BlockSpec((group, blk, blk), w_map(0)),
            pl.BlockSpec((group, blk, blk), w_map(1)),
        ],
        out_specs=[
            whole((out_blocks, rows, blk)),
            whole((out_blocks, rows, blk)),
        ],
    )
    out_shape = [jax.ShapeDtypeStruct((out_blocks, rows, blk), jnp.float32)] * 2
    return pl.pallas_call(
        block_kernel(group, block_cols, pick_row, flips),
        grid_spec=spec,
        out_shape=out_shape,
        compiler_params=pltpu.CompilerParams(dimension_semantics=("arbitrary",)),
    )(codes0, codes1, counts, x0, x1, w0, w1)


def exchange_sum(x, axis):
    count = lax.axis_size(axis)
    me = lax.axis_index(axis)
    chunks = x.reshape((count, x.shape[0] // count) + x.shape[1:])
    total = chunks[me]
    for shift in range(1, count):
        sent = chunks[(me + shift) % count]
        pairs = [(i, (i + shift) % count) for i in range(count)]
        total = total + lax.ppermute(sent, axis, pairs)
    return total


def local(tokens, cotangent, up_values, up_index, up_count, down_values, down_index, down_count):
    block_size = up_values.shape[-1]
    tile_rows = tokens.shape[1]
    block_rows = tile_rows // block_size
    block_cols = FF // (block_size * lax.axis_size(("col", "seq")))
    up_vals = up_values[0, 0]
    up_codes = up_index[0, 0]
    down_vals = down_values[0, 0]
    down_codes = down_index[0, 0]
    first_counts = jnp.concatenate([up_count.reshape(1), down_count.reshape(1)])
    second_counts = jnp.concatenate([down_count.reshape(1), up_count.reshape(1)])

    stacked = jnp.stack([tokens, cotangent])
    local_rows = stacked.shape[1]
    blocked = stacked.reshape(2, local_rows, block_rows, block_size).transpose(0, 2, 1, 3)
    shard_rows = lax.all_gather(blocked, ("col", "seq"), axis=2, tiled=True)
    pre_part, grad_part = block_pass(
        shard_rows[0], up_vals, up_codes, shard_rows[1], down_vals, down_codes,
        first_counts, block_cols, True, block_cols, (False, True),
    )
    partial_value = jnp.stack([pre_part, grad_part])
    count_rows = partial_value.shape[2]
    partial_value = partial_value.transpose(2, 0, 1, 3).reshape(count_rows, 2, -1)
    shares = exchange_sum(partial_value, "row").transpose(1, 0, 2)
    activated = lax.all_gather(activate(shares), "row", axis=1, tiled=True)
    activated = activated.reshape(2, count_rows, block_cols, block_size).transpose(0, 2, 1, 3)
    out_part, back_part = block_pass(
        activated[0], down_vals, down_codes, activated[1], up_vals, up_codes,
        second_counts, block_cols, False, block_rows, (False, True),
    )
    final = jnp.stack([out_part, back_part]).transpose(2, 0, 1, 3).reshape(count_rows, 2, tile_rows)
    result = exchange_sum(final, ("col", "seq")).astype(jnp.bfloat16)
    return (result[:, 0], result[:, 1])


def solution(mesh):
    return jax.shard_map(
        local,
        mesh=mesh,
        in_specs=(
            P(("col", "seq"), "row"),
            P(("col", "seq"), "row"),
            P("row", ("col", "seq"), None, None, None),
            P("row", ("col", "seq"), None),
            P("row", ("col", "seq")),
            P("row", ("col", "seq"), None, None, None),
            P("row", ("col", "seq"), None),
            P("row", ("col", "seq")),
        ),
        out_specs=(P(("col", "seq"), "row"), P(("col", "seq"), "row")),
        check_vma=False,
    )
```

profile of v0, /device:TPU:0, one launch (start us, length us, event | category | flops | bytes accessed | tf_op | source)
XLA Modules:
  0.0 131.4 jit_solution(1922508254280045726)
XLA Ops:
  0.7 1.3 reduce.codes1.codes0
  2.0 1.3 reduce.1.codes0.codes1
  4.5 0.8 copy_bitcast_fusion.2
  5.3 11.0 %all_gather.6 = bf16[2,24,32,128]{3,1,0,2:T(8,128)(2,1)S(1)} all-gather(bf16[2,24,4,128]{3,1,0,2:T(8,128)(2,1)S(1)} %maximum_bitcast_fusion.2), channel_id=1, replica_groups=mesh['row'=4,'col'=4,'seq'=2] {'col','seq'}, dimensions={2}, use_global_device_ids=true | all-gather | bytes 442368 | tf_op jit(solution)/shard_map/all_gather | solution.py:139
  16.4 0.7 copy.39
  17.1 0.7 copy.38
  17.8 0.7 pad_add_fusion
  18.5 16.1 %shard_map.95 = (f32[48,32,128]{2,1,0:T(8,128)}, f32[48,32,128]{2,1,0:T(8,128)}) custom-call(s32[576]{0:T(1024)} %reduce.1.codes0.codes1, s32[576]{0:T(1024)} %reduce.codes1.codes0, s32[2]{0:T(128)} %get-tuple-element.29.counts, bf16[24,32,128]{2,1,0:T(8,128)(2,1)} %bitcast.105, bf16[24,32,128]{2,1,0:T(8,128)(2,1)} %bitcast.106, ...), custom_call_target="tpu_custom_call" | custom-call | tf_op jit(solution)/shard_map/pallas_call | solution.py:104
  34.6 1.5 %maximum_bitcast_fusion = f32[32,2,48,128]{3,0,2,1:T(8,128)S(1)} fusion(f32[1,48,32,128]{3,2,1,0:T(8,128)} %bitcast.108, f32[1,48,32,128]{3,2,1,0:T(8,128)} %bitcast.107), kind=kLoop, calls=%fused_computation | loop fusion | flops 393216 | bytes 3145728 | tf_op jit(solution)/shard_map/transpose | solution.py:146
  36.1 0.9 copy.21
  37.0 0.2 reshape_reshape.6
  37.3 0.1 dynamic-slice_bitcast_fusion.2
  37.4 5.3 %collective-permute-start.2 = (f32[8,2,6144]{2,0,1:T(8,128)S(1)}, f32[8,2,6144]{2,0,1:T(8,128)S(1)}, u32[]{:S(2)}, u32[]{:S(2)}) collective-permute-start(f32[8,2,6144]{2,0,1:T(8,128)S(1)} %get-tuple-element.11), channel_id=1, source_target_pairs={{0,24},{8,0},{16,8},{24,16},{1,25},{9,1},{17,9},{25,17},{2,26},{10... | collective-permute-start | bytes 1179656 | tf_op jit(solution)/shard_map/ppermute | solution.py:120
  42.7 0.0 collective-permute-start.1
  42.7 0.6 collective-permute-start
  43.4 9.0 %collective-permute-done.2 = f32[8,2,6144]{2,0,1:T(8,128)S(1)} collective-permute-done((f32[8,2,6144]{2,0,1:T(8,128)S(1)}, f32[8,2,6144]{2,0,1:T(8,128)S(1)}, u32[]{:S(2)}, u32[]{:S(2)}) %collective-permute-start.2) | collective-permute-done | bytes 393248 | tf_op jit(solution)/shard_map/ppermute | solution.py:120
  52.3 20.3 %collective-permute-done.1 = f32[8,2,6144]{2,0,1:T(8,128)S(1)} collective-permute-done((f32[8,2,6144]{2,0,1:T(8,128)S(1)}, f32[8,2,6144]{2,0,1:T(8,128)S(1)}, u32[]{:S(2)}, u32[]{:S(2)}) %collective-permute-start.1) | collective-permute-done | bytes 393248 | tf_op jit(solution)/shard_map/ppermute | solution.py:120
  72.6 0.0 collective-permute-done
  72.6 1.1 fusion.2
  73.6 0.1 multiply_convert_fusion
  73.8 21.4 %all_gather.7 = bf16[2,32,6144]{2,1,0:T(8,128)(2,1)S(1)} all-gather(bf16[2,8,6144]{2,1,0:T(8,128)(2,1)S(1)} %pad_maximum_fusion), channel_id=1, replica_groups=mesh['row'=4,'col'=4,'seq'=2] {'row'}, dimensions={1}, use_global_device_ids=true | all-gather | bytes 983040 | tf_op jit(solution)/shard_map/all_gather | solution.py:148
  95.2 0.1 bitcast_bitcast_fusion
  95.4 1.0 slice_bitcast_fusion
  96.3 16.7 %shard_map.96 = (f32[24,32,128]{2,1,0:T(8,128)}, f32[24,32,128]{2,1,0:T(8,128)}) custom-call(s32[576]{0:T(1024)} %reduce.codes1.codes0, s32[576]{0:T(1024)} %reduce.1.codes0.codes1, s32[2]{0:T(128)} %get-tuple-element.28.counts, bf16[48,32,128]{2,1,0:T(8,128)(2,1)} %get-tuple-element.21.x0, bf16[48,32,128]{2,1,0:T(8,128)(2,1)} %get-tuple-element.20.x1, ...), custom_call_target="tpu_custom_call" | custom-call | tf_op jit(solution)/shard_map/pallas_call | solution.py:104
  113.0 1.2 maximum_bitcast_fusion.1
  114.2 0.5 copy.23
  114.7 0.4 reshape_reshape.7
  115.1 0.1 dynamic-slice_bitcast_fusion.9
  115.2 0.1 collective-permute-start.9
  115.2 1.6 %collective-permute-start.8 = (f32[4,2,3072]{2,1,0:T(2,128)S(1)}, f32[4,2,3072]{2,1,0:T(2,128)S(1)}, u32[]{:S(2)}, u32[]{:S(2)}) collective-permute-start(f32[4,2,3072]{2,1,0:T(2,128)S(1)} %get-tuple-element.15), channel_id=1, source_target_pairs={{0,6},{1,7},{2,0},{3,1},{4,2},{5,3},{6,4},{7,5},{8,14},{9,15},{10,... | collective-permute-start | bytes 294920 | tf_op jit(solution)/shard_map/ppermute | solution.py:120
  116.8 2.2 %collective-permute-start.7 = (f32[4,2,3072]{2,1,0:T(2,128)S(1)}, f32[4,2,3072]{2,1,0:T(2,128)S(1)}, u32[]{:S(2)}, u32[]{:S(2)}) collective-permute-start(f32[4,2,3072]{2,1,0:T(2,128)S(1)} %get-tuple-element.16), channel_id=1, source_target_pairs={{0,5},{1,6},{2,7},{3,0},{4,1},{5,2},{6,3},{7,4},{8,13},{9,14},{10,... | collective-permute-start | bytes 294920 | tf_op jit(solution)/shard_map/ppermute | solution.py:120
  119.0 0.1 collective-permute-start.6
  119.1 1.4 %collective-permute-start.5 = (f32[4,2,3072]{2,1,0:T(2,128)S(1)}, f32[4,2,3072]{2,1,0:T(2,128)S(1)}, u32[]{:S(2)}, u32[]{:S(2)}) collective-permute-start(f32[4,2,3072]{2,1,0:T(2,128)S(1)} %get-tuple-element.18), channel_id=1, source_target_pairs={{0,3},{1,4},{2,5},{3,6},{4,7},{5,0},{6,1},{7,2},{8,11},{9,12},{10,... | collective-permute-start | bytes 294920 | tf_op jit(solution)/shard_map/ppermute | solution.py:120
  120.5 0.0 collective-permute-done.9
  120.5 2.8 %collective-permute-start.4 = (f32[4,2,3072]{2,1,0:T(2,128)S(1)}, f32[4,2,3072]{2,1,0:T(2,128)S(1)}, u32[]{:S(2)}, u32[]{:S(2)}) collective-permute-start(f32[4,2,3072]{2,1,0:T(2,128)S(1)} %get-tuple-element.19), channel_id=1, source_target_pairs={{0,2},{1,3},{2,4},{3,5},{4,6},{5,7},{6,0},{7,1},{8,10},{9,11},{10,... | collective-permute-start | bytes 294920 | tf_op jit(solution)/shard_map/ppermute | solution.py:120
  123.3 0.0 collective-permute-done.8
  123.3 0.5 collective-permute-start.3
  123.9 0.0 collective-permute-done.7
  123.9 0.3 collective-permute-done.6
  124.2 5.8 %collective-permute-done.5 = f32[4,2,3072]{2,1,0:T(2,128)S(1)} collective-permute-done((f32[4,2,3072]{2,1,0:T(2,128)S(1)}, f32[4,2,3072]{2,1,0:T(2,128)S(1)}, u32[]{:S(2)}, u32[]{:S(2)}) %collective-permute-start.5) | collective-permute-done | bytes 98336 | tf_op jit(solution)/shard_map/ppermute | solution.py:120
  129.9 0.0 collective-permute-done.4
  129.9 0.0 collective-permute-done.3
  129.9 0.2 fusion.16
  130.1 0.1 fusion.18
  130.2 0.6 copy.41
  130.8 0.6 copy.40
  (3 shorter events, 0.1 us)
Async XLA Ops:
  37.4 14.9 %collective-permute-start.2 = (f32[8,2,6144]{2,0,1:T(8,128)S(1)}, f32[8,2,6144]{2,0,1:T(8,128)S(1)}, u32[]{:S(2)}, u32[]{:S(2)}) collective-permute-start(f32[8,2,6144]{2,0,1:T(8,128)S(1)} %get-tuple-element.11), channel_id=1, source_target_pairs={{0,24},{8,0},{16,8},{24,16},{1,25},{9,1},{17,9},{25,17},{2,26},{10... | collective-permute-start | bytes 1179656 | tf_op jit(solution)/shard_map/ppermute | solution.py:120
  42.7 29.9 %collective-permute-start.1 = (f32[8,2,6144]{2,0,1:T(8,128)S(1)}, f32[8,2,6144]{2,0,1:T(8,128)S(1)}, u32[]{:S(2)}, u32[]{:S(2)}) collective-permute-start(f32[8,2,6144]{2,0,1:T(8,128)S(1)} %get-tuple-element.12), channel_id=1, source_target_pairs={{0,16},{8,24},{16,0},{24,8},{1,17},{9,25},{17,1},{25,9},{2,18},{10... | collective-permute-start | bytes 1179656 | tf_op jit(solution)/shard_map/ppermute | solution.py:120
  42.7 29.9 %collective-permute-start = (f32[8,2,6144]{2,0,1:T(8,128)S(1)}, f32[8,2,6144]{2,0,1:T(8,128)}, u32[]{:S(2)}, u32[]{:S(2)}) collective-permute-start(f32[8,2,6144]{2,0,1:T(8,128)S(1)} %get-tuple-element.10), channel_id=1, source_target_pairs={{0,8},{8,16},{16,24},{24,0},{1,9},{9,17},{17,25},{25,1},{2,10},{10... | collective-permute-start | bytes 1179656 | tf_op jit(solution)/shard_map/ppermute | solution.py:120
  115.2 5.3 %collective-permute-start.9 = (f32[4,2,3072]{2,1,0:T(2,128)S(1)}, f32[4,2,3072]{2,1,0:T(2,128)S(1)}, u32[]{:S(2)}, u32[]{:S(2)}) collective-permute-start(f32[4,2,3072]{2,1,0:T(2,128)S(1)} %get-tuple-element.14), channel_id=1, source_target_pairs={{0,7},{1,0},{2,1},{3,2},{4,3},{5,4},{6,5},{7,6},{8,15},{9,8},{10,9... | collective-permute-start | bytes 294920 | tf_op jit(solution)/shard_map/ppermute | solution.py:120
  115.2 8.1 %collective-permute-start.8 = (f32[4,2,3072]{2,1,0:T(2,128)S(1)}, f32[4,2,3072]{2,1,0:T(2,128)S(1)}, u32[]{:S(2)}, u32[]{:S(2)}) collective-permute-start(f32[4,2,3072]{2,1,0:T(2,128)S(1)} %get-tuple-element.15), channel_id=1, source_target_pairs={{0,6},{1,7},{2,0},{3,1},{4,2},{5,3},{6,4},{7,5},{8,14},{9,15},{10,... | collective-permute-start | bytes 294920 | tf_op jit(solution)/shard_map/ppermute | solution.py:120
  116.8 7.1 %collective-permute-start.7 = (f32[4,2,3072]{2,1,0:T(2,128)S(1)}, f32[4,2,3072]{2,1,0:T(2,128)S(1)}, u32[]{:S(2)}, u32[]{:S(2)}) collective-permute-start(f32[4,2,3072]{2,1,0:T(2,128)S(1)} %get-tuple-element.16), channel_id=1, source_target_pairs={{0,5},{1,6},{2,7},{3,0},{4,1},{5,2},{6,3},{7,4},{8,13},{9,14},{10,... | collective-permute-start | bytes 294920 | tf_op jit(solution)/shard_map/ppermute | solution.py:120
  119.0 5.2 %collective-permute-start.6 = (f32[4,2,3072]{2,1,0:T(2,128)S(1)}, f32[4,2,3072]{2,1,0:T(2,128)S(1)}, u32[]{:S(2)}, u32[]{:S(2)}) collective-permute-start(f32[4,2,3072]{2,1,0:T(2,128)S(1)} %get-tuple-element.17), channel_id=1, source_target_pairs={{0,4},{1,5},{2,6},{3,7},{4,0},{5,1},{6,2},{7,3},{8,12},{9,13},{10,... | collective-permute-start | bytes 294920 | tf_op jit(solution)/shard_map/ppermute | solution.py:120
  119.1 10.8 %collective-permute-start.5 = (f32[4,2,3072]{2,1,0:T(2,128)S(1)}, f32[4,2,3072]{2,1,0:T(2,128)S(1)}, u32[]{:S(2)}, u32[]{:S(2)}) collective-permute-start(f32[4,2,3072]{2,1,0:T(2,128)S(1)} %get-tuple-element.18), channel_id=1, source_target_pairs={{0,3},{1,4},{2,5},{3,6},{4,7},{5,0},{6,1},{7,2},{8,11},{9,12},{10,... | collective-permute-start | bytes 294920 | tf_op jit(solution)/shard_map/ppermute | solution.py:120
  120.5 9.4 %collective-permute-start.4 = (f32[4,2,3072]{2,1,0:T(2,128)S(1)}, f32[4,2,3072]{2,1,0:T(2,128)S(1)}, u32[]{:S(2)}, u32[]{:S(2)}) collective-permute-start(f32[4,2,3072]{2,1,0:T(2,128)S(1)} %get-tuple-element.19), channel_id=1, source_target_pairs={{0,2},{1,3},{2,4},{3,5},{4,6},{5,7},{6,0},{7,1},{8,10},{9,11},{10,... | collective-permute-start | bytes 294920 | tf_op jit(solution)/shard_map/ppermute | solution.py:120
  123.3 6.6 %collective-permute-start.3 = (f32[4,2,3072]{2,1,0:T(2,128)S(1)}, f32[4,2,3072]{2,1,0:T(2,128)S(1)}, u32[]{:S(2)}, u32[]{:S(2)}) collective-permute-start(f32[4,2,3072]{2,1,0:T(2,128)S(1)} %get-tuple-element.13), channel_id=1, source_target_pairs={{0,1},{1,2},{2,3},{3,4},{4,5},{5,6},{6,7},{7,0},{8,9},{9,10},{10,1... | collective-permute-start | bytes 294920 | tf_op jit(solution)/shard_map/ppermute | solution.py:120
where the time goes:
time: 134 us; the launch traced here: 131 us
  waiting for transfers between devices  35.3 us (26%)
  Pallas kernels  32.8 us (24%)
  blocking collectives  32.5 us (24%)
  starting transfers between devices  14.7 us (11%)
  other arithmetic  7.31 us (5%)
  local copies, waits for them, and re-layouts  6.83 us (5%)
  between operations  2.1 us (2%)
    ppermute x10, waiting for transfers between devices, exchange_sum(): total = total + lax.ppermute(sent, axis, pairs)  35.3 us
    pallas_call x2, Pallas kernels, block_pass(): pl.pallas_call(block_kernel(group, block_cols, pick_row, flips), grid_spe...  32.8 us
    all_gather x1, blocking collectives, local(): activated = lax.all_gather(activate(shares), 'row', axis=1, tiled=True)  21.4 us
    ppermute x10, starting transfers between devices, exchange_sum(): total = total + lax.ppermute(sent, axis, pairs)  14.7 us
    all_gather x1, blocking collectives, local(): shard_rows = lax.all_gather(blocked, ('col', 'seq'), axis=2, tiled=True)  11 us
  transfers between devices with their start and end apart: 10, of which 4 were waited for; matrix products, arithmetic and copies ran while one was open for 0% of the time, Pallas kernels for 0%

commit v1 on v0

--- a/solution.py
+++ b/solution.py
@@ -151,8 +151,12 @@
         activated[0], down_vals, down_codes, activated[1], up_vals, up_codes,
         second_counts, block_cols, False, block_rows, (False, True),
     )
-    final = jnp.stack([out_part, back_part]).transpose(2, 0, 1, 3).reshape(count_rows, 2, tile_rows)
-    result = exchange_sum(final, ("col", "seq")).astype(jnp.bfloat16)
+    col_count = lax.axis_size("col")
+    seq_count = lax.axis_size("seq")
+    final = jnp.stack([out_part, back_part]).transpose(2, 0, 1, 3)
+    final = final.reshape(col_count, seq_count, local_rows, 2, tile_rows).transpose(1, 0, 2, 3, 4)
+    chip_sum = exchange_sum(final.reshape(count_rows, 2, tile_rows), "seq")
+    result = exchange_sum(chip_sum, "col").astype(jnp.bfloat16)
     return (result[:, 0], result[:, 1])
 
 

time: 134 us -> 131 us (0.978); the launches traced: 131 us -> 131 us
  starting transfers between devices: 14.7 us -> 6.83 us
  Pallas kernels: 32.8 us -> 38.1 us
  waiting for transfers between devices: 35.3 us -> 38.1 us
    ppermute x10 -> x7, starting transfers between devices: 14.7 us -> 6.83 us  [exchange_sum(): total = total + lax.ppermute(sent, axis, pairs)]
    pallas_call x2, Pallas kernels: 32.8 us -> 38.1 us  [block_pass(): pl.pallas_call(block_kernel(group, block_cols, pick_row, flips), grid_spe...]
    ppermute x10 -> x7, waiting for transfers between devices: 35.3 us -> 38.1 us  [exchange_sum(): total = total + lax.ppermute(sent, axis, pairs)]
  transfers between devices with their start and end apart: 10 -> 7, of which waited for: 4 -> 6; matrix products, arithmetic and copies ran while one was open for 0% -> 0% of each run, Pallas kernels for 0% -> 0%
where the time goes in v1:
time: 131 us
  Pallas kernels  38.1 us (29%)
  waiting for transfers between devices  38.1 us (29%)
  blocking collectives  31.4 us (24%)
  other arithmetic  7.41 us (6%)
  local copies, waits for them, and re-layouts  6.84 us (5%)
  starting transfers between devices  6.83 us (5%)
  between operations  2.18 us (2%)
    pallas_call x2, Pallas kernels, block_pass(): pl.pallas_call(block_kernel(group, block_cols, pick_row, flips), grid_spe...  38.1 us
    ppermute x7, waiting for transfers between devices, exchange_sum(): total = total + lax.ppermute(sent, axis, pairs)  38.1 us
    all_gather x1, blocking collectives, local(): activated = lax.all_gather(activate(shares), 'row', axis=1, tiled=True)  20.4 us
    all_gather x1, blocking collectives, local(): shard_rows = lax.all_gather(blocked, ('col', 'seq'), axis=2, tiled=True)  11 us
    ppermute x7, starting transfers between devices, exchange_sum(): total = total + lax.ppermute(sent, axis, pairs)  6.83 us
    unnamed x4, local copies, waits for them, and re-layouts  2.64 us
  transfers between devices with their start and end apart: 7, of which 6 were waited for; matrix products, arithmetic and copies ran while one was open for 0% of the time, Pallas kernels for 0%

profile of v1, /device:TPU:0, one launch (start us, length us, event | category | flops | bytes accessed | tf_op | source)
XLA Modules:
  0.0 130.9 jit_solution(4384561052513266105)
XLA Ops:
  0.7 1.3 reduce.codes1.codes0
  2.0 1.3 reduce.1.codes0.codes1
  4.5 0.8 copy_bitcast_fusion.2
  5.3 11.0 %all_gather.6 = bf16[2,24,32,128]{3,1,0,2:T(8,128)(2,1)S(1)} all-gather(bf16[2,24,4,128]{3,1,0,2:T(8,128)(2,1)S(1)} %maximum_bitcast_fusion.2), channel_id=1, replica_groups=mesh['row'=4,'col'=4,'seq'=2] {'col','seq'}, dimensions={2}, use_global_device_ids=true | all-gather | bytes 442368 | tf_op jit(solution)/shard_map/all_gather | solution.py:139
  16.4 0.7 copy.43
  17.1 0.7 copy.42
  17.8 0.6 pad_add_fusion
  18.5 18.8 %shard_map.95 = (f32[48,32,128]{2,1,0:T(8,128)}, f32[48,32,128]{2,1,0:T(8,128)}) custom-call(s32[576]{0:T(1024)} %reduce.1.codes0.codes1, s32[576]{0:T(1024)} %reduce.codes1.codes0, s32[2]{0:T(128)} %get-tuple-element.25.counts, bf16[24,32,128]{2,1,0:T(8,128)(2,1)} %bitcast.101, bf16[24,32,128]{2,1,0:T(8,128)(2,1)} %bitcast.102, ...), custom_call_target="tpu_custom_call" | custom-call | tf_op jit(solution)/shard_map/pallas_call | solution.py:104
  37.2 1.5 %maximum_bitcast_fusion = f32[32,2,48,128]{3,0,2,1:T(8,128)S(1)} fusion(f32[1,48,32,128]{3,2,1,0:T(8,128)} %bitcast.104, f32[1,48,32,128]{3,2,1,0:T(8,128)} %bitcast.103), kind=kLoop, calls=%fused_computation | loop fusion | flops 393216 | bytes 3145728 | tf_op jit(solution)/shard_map/transpose | solution.py:146
  38.7 0.9 copy.24
  39.6 0.2 reshape_reshape.6
  39.9 0.1 dynamic-slice_bitcast_fusion.3
  40.0 0.1 collective-permute-start.2
  40.0 0.1 collective-permute-start.1
  40.1 1.9 %collective-permute-start = (f32[8,2,6144]{2,0,1:T(8,128)S(1)}, f32[8,2,6144]{2,0,1:T(8,128)}, u32[]{:S(2)}, u32[]{:S(2)}) collective-permute-start(f32[8,2,6144]{2,0,1:T(8,128)S(1)} %get-tuple-element.10), channel_id=1, source_target_pairs={{0,8},{8,16},{16,24},{24,0},{1,9},{9,17},{17,25},{25,1},{2,10},{10... | collective-permute-start | bytes 1179656 | tf_op jit(solution)/shard_map/ppermute | solution.py:120
  42.1 10.1 %collective-permute-done.2 = f32[8,2,6144]{2,0,1:T(8,128)S(1)} collective-permute-done((f32[8,2,6144]{2,0,1:T(8,128)S(1)}, f32[8,2,6144]{2,0,1:T(8,128)S(1)}, u32[]{:S(2)}, u32[]{:S(2)}) %collective-permute-start.2) | collective-permute-done | bytes 393248 | tf_op jit(solution)/shard_map/ppermute | solution.py:120
  52.2 21.0 %collective-permute-done.1 = f32[8,2,6144]{2,0,1:T(8,128)S(1)} collective-permute-done((f32[8,2,6144]{2,0,1:T(8,128)S(1)}, f32[8,2,6144]{2,0,1:T(8,128)S(1)}, u32[]{:S(2)}, u32[]{:S(2)}) %collective-permute-start.1) | collective-permute-done | bytes 393248 | tf_op jit(solution)/shard_map/ppermute | solution.py:120
  73.1 0.0 collective-permute-done
  73.1 1.1 fusion.2
  74.2 0.1 multiply_convert_fusion
  74.4 20.4 %all_gather.7 = bf16[2,32,6144]{2,1,0:T(8,128)(2,1)S(1)} all-gather(bf16[2,8,6144]{2,1,0:T(8,128)(2,1)S(1)} %pad_maximum_fusion), channel_id=1, replica_groups=mesh['row'=4,'col'=4,'seq'=2] {'row'}, dimensions={1}, use_global_device_ids=true | all-gather | bytes 983040 | tf_op jit(solution)/shard_map/all_gather | solution.py:148
  94.8 0.1 bitcast_bitcast_fusion
  94.9 0.9 slice_bitcast_fusion
  95.9 19.4 %shard_map.96 = (f32[24,32,128]{2,1,0:T(8,128)}, f32[24,32,128]{2,1,0:T(8,128)}) custom-call(s32[576]{0:T(1024)} %reduce.codes1.codes0, s32[576]{0:T(1024)} %reduce.1.codes0.codes1, s32[2]{0:T(128)} %get-tuple-element.24.counts, bf16[48,32,128]{2,1,0:T(8,128)(2,1)} %get-tuple-element.14.x0, bf16[48,32,128]{2,1,0:T(8,128)(2,1)} %get-tuple-element.13.x1, ...), custom_call_target="tpu_custom_call" | custom-call | tf_op jit(solution)/shard_map/pallas_call | solution.py:104
  115.2 1.2 maximum_bitcast_fusion.1
  116.4 0.5 copy.26
  116.9 0.4 reshape.29
  117.3 0.1 copy.27
  117.4 0.1 collective-permute-start.3
  117.5 1.7 %collective-permute-done.3 = f32[16,2,3072]{2,1,0:T(2,128)S(1)} collective-permute-done((f32[16,2,3072]{2,1,0:T(2,128)S(1)}, f32[16,2,3072]{2,1,0:T(2,128)S(1)}, u32[]{:S(2)}, u32[]{:S(2)}) %collective-permute-start.3) | collective-permute-done | bytes 393248 | tf_op jit(solution)/shard_map/ppermute | solution.py:120
  119.2 0.2 bitcast_add_fusion
  119.4 0.5 collective-permute-start.6
  120.0 4.0 %collective-permute-start.5 = (f32[4,2,3072]{2,1,0:T(2,128)S(1)}, f32[4,2,3072]{2,1,0:T(2,128)S(1)}, u32[]{:S(2)}, u32[]{:S(2)}) collective-permute-start(f32[4,2,3072]{2,1,0:T(2,128)S(1)} %get-tuple-element.17), channel_id=1, source_target_pairs={{0,4},{2,6},{4,0},{6,2},{1,5},{3,7},{5,1},{7,3},{8,12},{10,14},{12... | collective-permute-start | bytes 294920 | tf_op jit(solution)/shard_map/ppermute | solution.py:120
  124.0 0.2 collective-permute-start.4
  124.1 1.5 %collective-permute-done.6 = f32[4,2,3072]{2,1,0:T(2,128)S(1)} collective-permute-done((f32[4,2,3072]{2,1,0:T(2,128)S(1)}, f32[4,2,3072]{2,1,0:T(2,128)S(1)}, u32[]{:S(2)}, u32[]{:S(2)}) %collective-permute-start.6) | collective-permute-done | bytes 98336 | tf_op jit(solution)/shard_map/ppermute | solution.py:120
  125.6 2.5 %collective-permute-done.5 = f32[4,2,3072]{2,1,0:T(2,128)S(1)} collective-permute-done((f32[4,2,3072]{2,1,0:T(2,128)S(1)}, f32[4,2,3072]{2,1,0:T(2,128)S(1)}, u32[]{:S(2)}, u32[]{:S(2)}) %collective-permute-start.5) | collective-permute-done | bytes 98336 | tf_op jit(solution)/shard_map/ppermute | solution.py:120
  128.2 1.3 %collective-permute-done.4 = f32[4,2,3072]{2,1,0:T(2,128)S(1)} collective-permute-done((f32[4,2,3072]{2,1,0:T(2,128)S(1)}, f32[4,2,3072]{2,1,0:T(2,128)S(1)}, u32[]{:S(2)}, u32[]{:S(2)}) %collective-permute-start.4) | collective-permute-done | bytes 98336 | tf_op jit(solution)/shard_map/ppermute | solution.py:120
  129.5 0.1 fusion.12
  129.6 0.1 fusion.14
  129.7 0.6 copy.45
  130.3 0.6 copy.44
  (5 shorter events, 0.1 us)
Async XLA Ops:
  40.0 12.2 %collective-permute-start.2 = (f32[8,2,6144]{2,0,1:T(8,128)S(1)}, f32[8,2,6144]{2,0,1:T(8,128)S(1)}, u32[]{:S(2)}, u32[]{:S(2)}) collective-permute-start(f32[8,2,6144]{2,0,1:T(8,128)S(1)} %get-tuple-element.11), channel_id=1, source_target_pairs={{0,24},{8,0},{16,8},{24,16},{1,25},{9,1},{17,9},{25,17},{2,26},{10... | collective-permute-start | bytes 1179656 | tf_op jit(solution)/shard_map/ppermute | solution.py:120
  40.0 33.1 %collective-permute-start.1 = (f32[8,2,6144]{2,0,1:T(8,128)S(1)}, f32[8,2,6144]{2,0,1:T(8,128)S(1)}, u32[]{:S(2)}, u32[]{:S(2)}) collective-permute-start(f32[8,2,6144]{2,0,1:T(8,128)S(1)} %get-tuple-element.12), channel_id=1, source_target_pairs={{0,16},{8,24},{16,0},{24,8},{1,17},{9,25},{17,1},{25,9},{2,18},{10... | collective-permute-start | bytes 1179656 | tf_op jit(solution)/shard_map/ppermute | solution.py:120
  40.1 33.0 %collective-permute-start = (f32[8,2,6144]{2,0,1:T(8,128)S(1)}, f32[8,2,6144]{2,0,1:T(8,128)}, u32[]{:S(2)}, u32[]{:S(2)}) collective-permute-start(f32[8,2,6144]{2,0,1:T(8,128)S(1)} %get-tuple-element.10), channel_id=1, source_target_pairs={{0,8},{8,16},{16,24},{24,0},{1,9},{9,17},{17,25},{25,1},{2,10},{10... | collective-permute-start | bytes 1179656 | tf_op jit(solution)/shard_map/ppermute | solution.py:120
  117.4 1.8 %collective-permute-start.3 = (f32[16,2,3072]{2,1,0:T(2,128)S(1)}, f32[16,2,3072]{2,1,0:T(2,128)S(1)}, u32[]{:S(2)}, u32[]{:S(2)}) collective-permute-start(f32[16,2,3072]{2,1,0:T(2,128)S(1)} %dynamic-slice_bitcast_fusion), channel_id=1, source_target_pairs={{0,1},{1,0},{2,3},{3,2},{4,5},{5,4},{6,7},{7,6},{8,9},{9,8},{10,11... | collective-permute-start | bytes 1179656 | tf_op jit(solution)/shard_map/ppermute | solution.py:120
  119.4 6.2 %collective-permute-start.6 = (f32[4,2,3072]{2,1,0:T(2,128)S(1)}, f32[4,2,3072]{2,1,0:T(2,128)S(1)}, u32[]{:S(2)}, u32[]{:S(2)}) collective-permute-start(f32[4,2,3072]{2,1,0:T(2,128)S(1)} %get-tuple-element.16), channel_id=1, source_target_pairs={{0,6},{2,0},{4,2},{6,4},{1,7},{3,1},{5,3},{7,5},{8,14},{10,8},{12,... | collective-permute-start | bytes 294920 | tf_op jit(solution)/shard_map/ppermute | solution.py:120
  120.0 8.2 %collective-permute-start.5 = (f32[4,2,3072]{2,1,0:T(2,128)S(1)}, f32[4,2,3072]{2,1,0:T(2,128)S(1)}, u32[]{:S(2)}, u32[]{:S(2)}) collective-permute-start(f32[4,2,3072]{2,1,0:T(2,128)S(1)} %get-tuple-element.17), channel_id=1, source_target_pairs={{0,4},{2,6},{4,0},{6,2},{1,5},{3,7},{5,1},{7,3},{8,12},{10,14},{12... | collective-permute-start | bytes 294920 | tf_op jit(solution)/shard_map/ppermute | solution.py:120
  124.0 5.5 %collective-permute-start.4 = (f32[4,2,3072]{2,1,0:T(2,128)S(1)}, f32[4,2,3072]{2,1,0:T(2,128)S(1)}, u32[]{:S(2)}, u32[]{:S(2)}) collective-permute-start(f32[4,2,3072]{2,1,0:T(2,128)S(1)} %get-tuple-element.15), channel_id=1, source_target_pairs={{0,2},{2,4},{4,6},{6,0},{1,3},{3,5},{5,7},{7,1},{8,10},{10,12},{12... | collective-permute-start | bytes 294920 | tf_op jit(solution)/shard_map/ppermute | solution.py:120

commit v2 on v1

--- a/solution.py
+++ b/solution.py
@@ -35,7 +35,7 @@
 
 
 def block_kernel(group, block_cols, pick_row, flips):
-    def kernel(codes0, codes1, counts, x0, x1, w0, w1, o0, o1):
+    def kernel(codes0, codes1, count0, count1, x, w0, w1, o0, o1):
         step = pl.program_id(0)
         first = step * group
 
@@ -44,18 +44,18 @@
             o0[...] = jnp.zeros_like(o0)
             o1[...] = jnp.zeros_like(o1)
 
-        streams = ((codes0, x0, w0, o0, flips[0], 0), (codes1, x1, w1, o1, flips[1], 1))
-        for codes, x, w, o, flipped, which in streams:
-            live = counts[which]
+        streams = ((codes0, count0, w0, o0, flips[0], 0), (codes1, count1, w1, o1, flips[1], 1))
+        for codes, count, w, o, flipped, which in streams:
+            live = count[0, 0]
 
             @pl.when(first < live)
-            def _(codes=codes, x=x, w=w, o=o, flipped=flipped, live=live):
+            def _(codes=codes, w=w, o=o, flipped=flipped, live=live, which=which):
                 for j in range(group):
                     slot = first + j
-                    code = codes[slot]
+                    code = codes[0, 0, slot]
                     row = lax.div(code, block_cols)
                     col = code - row * block_cols
-                    src = x[row if pick_row else col]
+                    src = x[which, row if pick_row else col]
                     blk = w[j]
                     if flipped:
                         prod = lax.dot_general(
@@ -71,27 +71,27 @@
     return kernel
 
 
-def block_pass(x0, w0, codes0, x1, w1, codes1, counts, block_cols, pick_row, out_blocks, flips):
+def block_pass(x, w0, codes0, count0, w1, codes1, count1, block_cols, pick_row, out_blocks, flips):
     slots, blk, _ = w0.shape
-    rows = x0.shape[1]
+    rows = x.shape[2]
     group = group_size(slots)
 
     def w_map(which):
-        def index_map(i, c0, c1, c):
-            last = jnp.maximum(c[which] - 1, 0) // group
+        def index_map(i, c0, c1, n0, n1):
+            live = (n0, n1)[which][0, 0]
+            last = jnp.maximum(live - 1, 0) // group
             return (jnp.minimum(i, last), 0, 0)
 
         return index_map
 
     def whole(shape):
-        return pl.BlockSpec(shape, lambda i, c0, c1, c: (0, 0, 0))
+        return pl.BlockSpec(shape, lambda i, *refs: (0,) * len(shape))
 
     spec = pltpu.PrefetchScalarGridSpec(
-        num_scalar_prefetch=3,
+        num_scalar_prefetch=4,
         grid=(slots // group,),
         in_specs=[
-            whole(x0.shape),
-            whole(x1.shape),
+            whole(x.shape),
             pl.BlockSpec((group, blk, blk), w_map(0)),
             pl.BlockSpec((group, blk, blk), w_map(1)),
         ],
@@ -106,7 +106,7 @@
         grid_spec=spec,
         out_shape=out_shape,
         compiler_params=pltpu.CompilerParams(dimension_semantics=("arbitrary",)),
-    )(codes0, codes1, counts, x0, x1, w0, w1)
+    )(codes0, codes1, count0, count1, x, w0, w1)
 
 
 def exchange_sum(x, axis):
@@ -127,19 +127,15 @@
     block_rows = tile_rows // block_size
     block_cols = FF // (block_size * lax.axis_size(("col", "seq")))
     up_vals = up_values[0, 0]
-    up_codes = up_index[0, 0]
     down_vals = down_values[0, 0]
-    down_codes = down_index[0, 0]
-    first_counts = jnp.concatenate([up_count.reshape(1), down_count.reshape(1)])
-    second_counts = jnp.concatenate([down_count.reshape(1), up_count.reshape(1)])
 
     stacked = jnp.stack([tokens, cotangent])
     local_rows = stacked.shape[1]
     blocked = stacked.reshape(2, local_rows, block_rows, block_size).transpose(0, 2, 1, 3)
     shard_rows = lax.all_gather(blocked, ("col", "seq"), axis=2, tiled=True)
     pre_part, grad_part = block_pass(
-        shard_rows[0], up_vals, up_codes, shard_rows[1], down_vals, down_codes,
-        first_counts, block_cols, True, block_cols, (False, True),
+        shard_rows, up_vals, up_index, up_count, down_vals, down_index, down_count,
+        block_cols, True, block_cols, (False, True),
     )
     partial_value = jnp.stack([pre_part, grad_part])
     count_rows = partial_value.shape[2]
@@ -148,8 +144,8 @@
     activated = lax.all_gather(activate(shares), "row", axis=1, tiled=True)
     activated = activated.reshape(2, count_rows, block_cols, block_size).transpose(0, 2, 1, 3)
     out_part, back_part = block_pass(
-        activated[0], down_vals, down_codes, activated[1], up_vals, up_codes,
-        second_counts, block_cols, False, block_rows, (False, True),
+        activated, down_vals, down_index, down_count, up_vals, up_index, up_count,
+        block_cols, False, block_rows, (False, True),
     )
     col_count = lax.axis_size("col")
     seq_count = lax.axis_size("seq")

time: 131 us -> 124 us (0.947); the launches traced: 131 us -> 122 us
  Pallas kernels: 38.1 us -> 26.6 us
  starting transfers between devices: 6.83 us -> 15.6 us
  waiting for transfers between devices: 38.1 us -> 31.4 us
  blocking collectives: 31.4 us -> 36.4 us
  other arithmetic: 7.41 us -> 4.2 us
    pallas_call x2, Pallas kernels: 38.1 us -> 26.6 us  [block_pass(): pl.pallas_call(block_kernel(group, block_cols, pick_row, flips), grid_spe...]
    ppermute x7, starting transfers between devices: 6.83 us -> 15.6 us  [exchange_sum(): total = total + lax.ppermute(sent, axis, pairs)]
    ppermute x7, waiting for transfers between devices: 38.1 us -> 31.4 us  [exchange_sum(): total = total + lax.ppermute(sent, axis, pairs)]
    all_gather x1, blocking collectives: 20.4 us -> 25.3 us  [local(): activated = lax.all_gather(activate(shares), 'row', axis=1, tiled=True)]
    unnamed x2 -> x0, other arithmetic: 2.57 us -> none
    unnamed x4 -> x2, local copies, waits for them, and re-layouts: 2.64 us -> 1.24 us
  transfers between devices with their start and end apart: 7 -> 7, of which waited for: 6 -> 5; matrix products, arithmetic and copies ran while one was open for 0% -> 0% of each run, Pallas kernels for 0% -> 0%
where the time goes in v2:
time: 124 us; the launch traced here: 122 us
  blocking collectives  36.4 us (29%)
  waiting for transfers between devices  31.4 us (25%)
  Pallas kernels  26.6 us (21%)
  starting transfers between devices  15.6 us (13%)
  local copies, waits for them, and re-layouts  6.19 us (5%)
  other arithmetic  4.2 us (3%)
  between operations  2.16 us (2%)
    ppermute x7, waiting for transfers between devices, exchange_sum(): total = total + lax.ppermute(sent, axis, pairs)  31.4 us
    pallas_call x2, Pallas kernels, block_pass(): pl.pallas_call(block_kernel(group, block_cols, pick_row, flips), grid_spe...  26.6 us
    all_gather x1, blocking collectives, local(): activated = lax.all_gather(activate(shares), 'row', axis=1, tiled=True)  25.3 us
    ppermute x7, starting transfers between devices, exchange_sum(): total = total + lax.ppermute(sent, axis, pairs)  15.6 us
    all_gather x1, blocking collectives, local(): shard_rows = lax.all_gather(blocked, ('col', 'seq'), axis=2, tiled=True)  11 us
  transfers between devices with their start and end apart: 7, of which 5 were waited for; matrix products, arithmetic and copies ran while one was open for 0% of the time, Pallas kernels for 0%

profile of v2, /device:TPU:0, one launch (start us, length us, event | category | flops | bytes accessed | tf_op | source)
XLA Modules:
  0.0 122.4 jit_solution(10900739493307362348)
XLA Ops:
  0.7 0.8 copy_bitcast_fusion
  1.5 11.0 %all_gather.6 = bf16[2,24,32,128]{3,1,0,2:T(8,128)(2,1)S(1)} all-gather(bf16[2,24,4,128]{3,1,0,2:T(8,128)(2,1)S(1)} %maximum_bitcast_fusion.2), channel_id=1, replica_groups=mesh['row'=4,'col'=4,'seq'=2] {'col','seq'}, dimensions={2}, use_global_device_ids=true | all-gather | bytes 442368 | tf_op jit(solution)/shard_map/all_gather | solution.py:135
  12.5 0.8 copy.22.x
  14.6 13.4 %shard_map.95 = (f32[48,32,128]{2,1,0:T(8,128)}, f32[48,32,128]{2,1,0:T(8,128)}) custom-call(s32[1,1,576]{2,1,0:T(1,128)} %codes1.3, s32[1,1,576]{2,1,0:T(1,128)} %codes0.3, s32[1,1]{1,0:T(1,128)S(6)} %copy.39.count0.count1, s32[1,1]{1,0:T(1,128)S(6)} %copy.40.count1.count0, bf16[2,24,32,128]{3,2,1,0:T(8,128)(2,1)} %copy.22.x, ...), custom_call_target="tpu_custom_call" | custom-call | tf_op jit(solution)/shard_map/pallas_call | solution.py:104
  28.0 1.5 %maximum_bitcast_fusion = f32[32,2,48,128]{3,0,2,1:T(8,128)S(1)} fusion(f32[1,48,32,128]{3,2,1,0:T(8,128)} %bitcast.88, f32[1,48,32,128]{3,2,1,0:T(8,128)} %bitcast.87), kind=kLoop, calls=%fused_computation | loop fusion | flops 393216 | bytes 3145728 | tf_op jit(solution)/shard_map/transpose | solution.py:142
  29.5 0.9 copy.23
  30.4 0.2 reshape_reshape.6
  30.7 0.1 dynamic-slice_bitcast_fusion.3
  30.8 0.1 collective-permute-start
  30.8 5.1 %collective-permute-start.1 = (f32[8,2,6144]{2,0,1:T(8,128)S(1)}, f32[8,2,6144]{2,0,1:T(8,128)S(1)}, u32[]{:S(2)}, u32[]{:S(2)}) collective-permute-start(f32[8,2,6144]{2,0,1:T(8,128)S(1)} %get-tuple-element.12), channel_id=1, source_target_pairs={{0,16},{8,24},{16,0},{24,8},{1,17},{9,25},{17,1},{25,9},{2,18},{10... | collective-permute-start | bytes 1179656 | tf_op jit(solution)/shard_map/ppermute | solution.py:120
  35.9 0.0 collective-permute-start.2
  35.9 7.0 %collective-permute-done = f32[8,2,6144]{2,0,1:T(8,128)S(1)} collective-permute-done((f32[8,2,6144]{2,0,1:T(8,128)S(1)}, f32[8,2,6144]{2,0,1:T(8,128)S(1)}, u32[]{:S(2)}, u32[]{:S(2)}) %collective-permute-start) | collective-permute-done | bytes 393248 | tf_op jit(solution)/shard_map/ppermute | solution.py:120
  42.9 19.2 %collective-permute-done.1 = f32[8,2,6144]{2,0,1:T(8,128)S(1)} collective-permute-done((f32[8,2,6144]{2,0,1:T(8,128)S(1)}, f32[8,2,6144]{2,0,1:T(8,128)S(1)}, u32[]{:S(2)}, u32[]{:S(2)}) %collective-permute-start.1) | collective-permute-done | bytes 393248 | tf_op jit(solution)/shard_map/ppermute | solution.py:120
  62.1 0.0 collective-permute-done.2
  62.1 1.1 fusion.2
  63.2 0.1 multiply_convert_fusion
  63.4 25.3 %all_gather.7 = bf16[2,32,6144]{2,1,0:T(8,128)(2,1)S(1)} all-gather(bf16[2,8,6144]{2,1,0:T(8,128)(2,1)S(1)} %pad_maximum_fusion), channel_id=1, replica_groups=mesh['row'=4,'col'=4,'seq'=2] {'row'}, dimensions={1}, use_global_device_ids=true | all-gather | bytes 983040 | tf_op jit(solution)/shard_map/all_gather | solution.py:144
  88.7 1.0 bitcast_bitcast_fusion.x
  89.7 13.2 %shard_map.96 = (f32[24,32,128]{2,1,0:T(8,128)}, f32[24,32,128]{2,1,0:T(8,128)}) custom-call(s32[1,1,576]{2,1,0:T(1,128)} %codes0.3, s32[1,1,576]{2,1,0:T(1,128)} %codes1.3, s32[1,1]{1,0:T(1,128)S(6)} %copy.40.count1.count0, s32[1,1]{1,0:T(1,128)S(6)} %copy.39.count0.count1, bf16[2,48,32,128]{3,2,1,0:T(8,128)(2,1)} %bitcast_bitcast_fusion.x, ...), custom_call_target="tpu_custom_call" | custom-call | tf_op jit(solution)/shard_map/pallas_call | solution.py:104
  102.9 1.2 maximum_bitcast_fusion.1
  104.1 0.5 copy.25
  104.6 0.4 reshape.19
  105.0 0.1 copy.26
  105.1 0.1 collective-permute-start.3
  105.2 1.7 %collective-permute-done.3 = f32[16,2,3072]{2,1,0:T(2,128)S(1)} collective-permute-done((f32[16,2,3072]{2,1,0:T(2,128)S(1)}, f32[16,2,3072]{2,1,0:T(2,128)S(1)}, u32[]{:S(2)}, u32[]{:S(2)}) %collective-permute-start.3) | collective-permute-done | bytes 393248 | tf_op jit(solution)/shard_map/ppermute | solution.py:120
  106.9 0.2 bitcast_add_fusion
  107.1 1.9 %collective-permute-start.4 = (f32[4,2,3072]{2,1,0:T(2,128)S(1)}, f32[4,2,3072]{2,1,0:T(2,128)S(1)}, u32[]{:S(2)}, u32[]{:S(2)}) collective-permute-start(f32[4,2,3072]{2,1,0:T(2,128)S(1)} %get-tuple-element.13), channel_id=1, source_target_pairs={{0,2},{2,4},{4,6},{6,0},{1,3},{3,5},{5,7},{7,1},{8,10},{10,12},{12... | collective-permute-start | bytes 294920 | tf_op jit(solution)/shard_map/ppermute | solution.py:120
  109.0 5.7 %collective-permute-start.5 = (f32[4,2,3072]{2,1,0:T(2,128)S(1)}, f32[4,2,3072]{2,1,0:T(2,128)S(1)}, u32[]{:S(2)}, u32[]{:S(2)}) collective-permute-start(f32[4,2,3072]{2,1,0:T(2,128)S(1)} %get-tuple-element.15), channel_id=1, source_target_pairs={{0,4},{2,6},{4,0},{6,2},{1,5},{3,7},{5,1},{7,3},{8,12},{10,14},{12... | collective-permute-start | bytes 294920 | tf_op jit(solution)/shard_map/ppermute | solution.py:120
  114.7 2.8 %collective-permute-start.6 = (f32[4,2,3072]{2,1,0:T(2,128)S(1)}, f32[4,2,3072]{2,1,0:T(2,128)S(1)}, u32[]{:S(2)}, u32[]{:S(2)}) collective-permute-start(f32[4,2,3072]{2,1,0:T(2,128)S(1)} %get-tuple-element.14), channel_id=1, source_target_pairs={{0,6},{2,0},{4,2},{6,4},{1,7},{3,1},{5,3},{7,5},{8,14},{10,8},{12,... | collective-permute-start | bytes 294920 | tf_op jit(solution)/shard_map/ppermute | solution.py:120
  117.5 0.0 collective-permute-done.4
  117.5 1.6 %collective-permute-done.5 = f32[4,2,3072]{2,1,0:T(2,128)S(1)} collective-permute-done((f32[4,2,3072]{2,1,0:T(2,128)S(1)}, f32[4,2,3072]{2,1,0:T(2,128)S(1)}, u32[]{:S(2)}, u32[]{:S(2)}) %collective-permute-start.5) | collective-permute-done | bytes 98336 | tf_op jit(solution)/shard_map/ppermute | solution.py:120
  119.2 1.9 %collective-permute-done.6 = f32[4,2,3072]{2,1,0:T(2,128)S(1)} collective-permute-done((f32[4,2,3072]{2,1,0:T(2,128)S(1)}, f32[4,2,3072]{2,1,0:T(2,128)S(1)}, u32[]{:S(2)}, u32[]{:S(2)}) %collective-permute-start.6) | collective-permute-done | bytes 98336 | tf_op jit(solution)/shard_map/ppermute | solution.py:120
  121.0 0.1 fusion.12
  121.1 0.1 fusion.13
  121.2 0.6 copy.37
  121.8 0.6 copy.38
  (4 shorter events, 0.1 us)
Async XLA Ops:
  30.8 12.1 %collective-permute-start = (f32[8,2,6144]{2,0,1:T(8,128)S(1)}, f32[8,2,6144]{2,0,1:T(8,128)S(1)}, u32[]{:S(2)}, u32[]{:S(2)}) collective-permute-start(f32[8,2,6144]{2,0,1:T(8,128)S(1)} %get-tuple-element.10), channel_id=1, source_target_pairs={{0,8},{8,16},{16,24},{24,0},{1,9},{9,17},{17,25},{25,1},{2,10},{10... | collective-permute-start | bytes 1179656 | tf_op jit(solution)/shard_map/ppermute | solution.py:120
  30.8 31.3 %collective-permute-start.1 = (f32[8,2,6144]{2,0,1:T(8,128)S(1)}, f32[8,2,6144]{2,0,1:T(8,128)S(1)}, u32[]{:S(2)}, u32[]{:S(2)}) collective-permute-start(f32[8,2,6144]{2,0,1:T(8,128)S(1)} %get-tuple-element.12), channel_id=1, source_target_pairs={{0,16},{8,24},{16,0},{24,8},{1,17},{9,25},{17,1},{25,9},{2,18},{10... | collective-permute-start | bytes 1179656 | tf_op jit(solution)/shard_map/ppermute | solution.py:120
  35.9 26.2 %collective-permute-start.2 = (f32[8,2,6144]{2,0,1:T(8,128)S(1)}, f32[8,2,6144]{2,0,1:T(8,128)}, u32[]{:S(2)}, u32[]{:S(2)}) collective-permute-start(f32[8,2,6144]{2,0,1:T(8,128)S(1)} %get-tuple-element.11), channel_id=1, source_target_pairs={{0,24},{8,0},{16,8},{24,16},{1,25},{9,1},{17,9},{25,17},{2,26},{10... | collective-permute-start | bytes 1179656 | tf_op jit(solution)/shard_map/ppermute | solution.py:120
  105.1 1.8 %collective-permute-start.3 = (f32[16,2,3072]{2,1,0:T(2,128)S(1)}, f32[16,2,3072]{2,1,0:T(2,128)S(1)}, u32[]{:S(2)}, u32[]{:S(2)}) collective-permute-start(f32[16,2,3072]{2,1,0:T(2,128)S(1)} %dynamic-slice_bitcast_fusion), channel_id=1, source_target_pairs={{0,1},{1,0},{2,3},{3,2},{4,5},{5,4},{6,7},{7,6},{8,9},{9,8},{10,11... | collective-permute-start | bytes 1179656 | tf_op jit(solution)/shard_map/ppermute | solution.py:120
  107.1 10.4 %collective-permute-start.4 = (f32[4,2,3072]{2,1,0:T(2,128)S(1)}, f32[4,2,3072]{2,1,0:T(2,128)S(1)}, u32[]{:S(2)}, u32[]{:S(2)}) collective-permute-start(f32[4,2,3072]{2,1,0:T(2,128)S(1)} %get-tuple-element.13), channel_id=1, source_target_pairs={{0,2},{2,4},{4,6},{6,0},{1,3},{3,5},{5,7},{7,1},{8,10},{10,12},{12... | collective-permute-start | bytes 294920 | tf_op jit(solution)/shard_map/ppermute | solution.py:120
  109.0 10.1 %collective-permute-start.5 = (f32[4,2,3072]{2,1,0:T(2,128)S(1)}, f32[4,2,3072]{2,1,0:T(2,128)S(1)}, u32[]{:S(2)}, u32[]{:S(2)}) collective-permute-start(f32[4,2,3072]{2,1,0:T(2,128)S(1)} %get-tuple-element.15), channel_id=1, source_target_pairs={{0,4},{2,6},{4,0},{6,2},{1,5},{3,7},{5,1},{7,3},{8,12},{10,14},{12... | collective-permute-start | bytes 294920 | tf_op jit(solution)/shard_map/ppermute | solution.py:120
  114.7 6.3 %collective-permute-start.6 = (f32[4,2,3072]{2,1,0:T(2,128)S(1)}, f32[4,2,3072]{2,1,0:T(2,128)S(1)}, u32[]{:S(2)}, u32[]{:S(2)}) collective-permute-start(f32[4,2,3072]{2,1,0:T(2,128)S(1)} %get-tuple-element.14), channel_id=1, source_target_pairs={{0,6},{2,0},{4,2},{6,4},{1,7},{3,1},{5,3},{7,5},{8,14},{10,8},{12,... | collective-permute-start | bytes 294920 | tf_op jit(solution)/shard_map/ppermute | solution.py:120
